TPU v7x, 512 devices: a whole 4x8x8 slice. The times are simulated.
512 devices in a mesh: row: 32 (over z_hi, y), col: 16 (over x, z_lo, core).
Axes of the slice: x: 4, y: 8, z: 8 (z_hi: 4, z_lo: 2; z = z_hi * 2 + z_lo), core: 2. Of those that a mesh axis runs over, the one named last changes fastest.
Arguments:
- s_rows: bfloat16 [32768, 1024], P('row', 'col'), may hold values from -0.1875 to 0.1875
- iterate: bfloat16 [1024, 32768], P('row', 'col'), may hold values from -6 to 6
Outputs:
- product: bfloat16 [32768, 32768], P('row', 'col')
All inputs are finite; a program needn't handle non-finite values.
Results may differ from a plain program's by a relative error of at most 0.001.
Values may be sent and summed in bfloat16 or wider, within the bound.
No kernel may reach another device: no remote copies, remote signals or barrier semaphores. Data moves between devices by JAX's collectives and lax.ppermute only.
A program may use at most 64 MiB of HBM per device.

v0:
```python
import jax
import jax.numpy as jnp
from jax import lax
from jax.sharding import PartitionSpec as P


def shards(s_rows, iterate):
    panel_rows = lax.all_gather(s_rows, "col", axis=1, tiled=True)
    whole = lax.all_gather(iterate, "row", axis=0, tiled=True)
    product = jnp.dot(panel_rows, whole, preferred_element_type=jnp.float32)
    return product.astype(jnp.bfloat16)


def solution(mesh):
    return jax.shard_map(
        shards,
        mesh=mesh,
        in_specs=(P("row", "col"), P("row", "col")),
        out_specs=P("row", "col"),
        check_vma=False,
    )
```

profile of v0, /device:TPU:1, one launch (start us, length us, event | category | flops | bytes accessed | tf_op | source)
XLA Modules:
  0.0 174.7 jit_solution(2706381488308733073)
XLA Ops:
  6.5 0.0 all-gather.3.cloned.1.call-start
  6.5 0.7 all-gather.3.cloned.1.call-update
  7.3 0.0 all-gather.5.cloned.1.call-start
  7.3 0.7 all-gather.5.cloned.1.call-update
  8.0 46.6 %all-gather.3.cloned.1.call-done = bf16[1024,1024]{0,1:T(8,128)(2,1)} async-done(((bf16[1024,64]{0,1:T(8,128)(2,1)}), bf16[1024,1024]{0,1:T(8,128)(2,1)}) %all-gather.3.cloned.1.call-update) | async-done | bytes 2097168 | tf_op jit(solution)/shard_map/all_gather | solution.py:8
  54.6 103.8 %all-gather.5.cloned.1.call-done = bf16[1024,2048]{1,0:T(8,128)(2,1)} async-done(((bf16[32,2048]{1,0:T(8,128)(2,1)}), bf16[1024,2048]{1,0:T(8,128)(2,1)}) %all-gather.5.cloned.1.call-update) | async-done | bytes 4194320 | tf_op jit(solution)/shard_map/all_gather | solution.py:9
  158.4 9.4 %convolution_convert_fusion = bf16[1024,2048]{1,0:T(8,128)(2,1)} fusion(bf16[1024,1024]{0,1:T(8,128)(2,1)} %all-gather.3.cloned.1.call-done, bf16[1024,2048]{1,0:T(8,128)(2,1)} %all-gather.5.cloned.1.call-done), kind=kOutput, calls=%fused_computation | convolution fusion | flops 4297064448 | bytes 10485760 | tf_op jit(solution)/shard_map/dot_general | solution.py:10
Async XLA Ops:
  6.5 48.1 %all-gather.3.cloned.1.call-start = ((), (), s32[]{:S(2)}) async-start(), calls=%async_computation | async-start | bytes 2228224 | tf_op jit(solution)/shard_map/all_gather | solution.py:8
  7.3 151.2 %all-gather.5.cloned.1.call-start = ((), (), s32[]{:S(2)}) async-start(), calls=%async_computation.1 | async-start | bytes 4325376 | tf_op jit(solution)/shard_map/all_gather | solution.py:9
Sparse Core Ops, SparseCore 0:
  9.5 45.0 all-gather.2
  57.8 100.6 all-gather.4
where the time goes:
time: 176 us; the launch traced here: 175 us
  waiting for transfers between devices  152 us (86%)
  between operations  13.4 us (8%)
  matrix products  9.41 us (5%)
    all_gather x1, waiting for transfers between devices, shards(): whole = lax.all_gather(iterate, 'row', axis=0, tiled=True)  104 us
    all_gather x1, waiting for transfers between devices, shards(): panel_rows = lax.all_gather(s_rows, 'col', axis=1, tiled=True)  46.6 us
    dot_general x1, matrix products, shards(): product = jnp.dot(panel_rows, whole, preferred_element_type=jnp.float32)  9.41 us
  transfers between devices with their start and end apart: 2, of which 2 were waited for; matrix products, arithmetic and copies ran while one was open for 0% of the time, Pallas kernels for 0%

commit v1 on v0

v1 whole, which is shorter than its diff:
```python
import jax
import jax.numpy as jnp
from jax import lax
from jax.sharding import Mesh, PartitionSpec as P

ROW = ("z_hi", "y")
COL = ("x", "z_lo", "core")


def shards(s_rows, iterate):
    panel = lax.all_gather(s_rows, COL, axis=1, tiled=True)
    nz, ny = lax.axis_size("z_hi"), lax.axis_size("y")
    w = lax.all_gather(iterate, "z_hi", axis=0, tiled=False)
    w = lax.all_gather(w, "y", axis=0, tiled=False)
    s4 = panel.reshape(panel.shape[0], nz, ny, -1)
    product = jnp.einsum("rzyk,yzkc->rc", s4, w, preferred_element_type=jnp.float32)
    return product.astype(jnp.bfloat16)


def solution(mesh):
    nr, nc = mesh.devices.shape
    devs = mesh.devices.reshape(4, nr // 4, nc // 4, 2, 2)
    m = Mesh(devs, ROW + COL)
    return jax.shard_map(shards, mesh=m, in_specs=(P(ROW, COL), P(ROW, COL)), out_specs=P(ROW, COL), check_vma=False)
```

time: 176 us -> 129 us (0.73)
  waiting for transfers between devices: 152 us -> 84.8 us
  blocking collectives: 0 us -> 21.6 us
    all_gather x2, waiting for transfers between devices: 150 us -> 84 us  [the longest x1 58.3 us: shards(): w = lax.all_gather(w, 'y', axis=0, tiled=False)]
    all_gather x0 -> x1, blocking collectives: none -> 21.6 us  [shards(): w = lax.all_gather(iterate, 'z_hi', axis=0, tiled=False)]
where the time goes in v1:
time: 129 us
  waiting for transfers between devices  84.8 us (66%)
  blocking collectives  21.6 us (17%)
  between operations  13.4 us (10%)
  matrix products  9.41 us (7%)
    all_gather x1, waiting for transfers between devices, shards(): w = lax.all_gather(w, 'y', axis=0, tiled=False)  58.3 us
    all_gather x1, waiting for transfers between devices, shards(): panel = lax.all_gather(s_rows, COL, axis=1, tiled=True)  25.8 us
    all_gather x1, blocking collectives, shards(): w = lax.all_gather(iterate, 'z_hi', axis=0, tiled=False)  21.6 us
    dot_general x1, matrix products, shards(): jnp.einsum('rzyk,yzkc->rc', s4, w, preferred_element_type=jnp.float32)  9.41 us
  transfers between devices with their start and end apart: 2, of which 2 were waited for; matrix products, arithmetic and copies ran while one was open for 0% of the time, Pallas kernels for 0%

profile of v1, /device:TPU:1, one launch (start us, length us, event | category | flops | bytes accessed | tf_op | source)
XLA Modules:
  0.0 129.2 jit_solution(9073005861399664550)
XLA Ops:
  6.5 0.0 all-gather.5.cloned.1.call-start
  6.5 0.7 all-gather.5.cloned.1.call-update
  7.3 0.0 all-gather.7.cloned.1.call-start
  7.3 21.6 %all-gather = bf16[128,2048]{1,0:T(8,128)(2,1)} all-gather(bf16[32,2048]{1,0:T(8,128)(2,1)} %param.3), channel_id=2, replica_groups=mesh['z_hi'=4,'y'=8,'x'=4,'z_lo'=2,'core'=2] {'z_hi'}, dimensions={0}, use_global_device_ids=true | all-gather | bytes 655360 | tf_op jit(solution)/shard_map/all_gather | solution.py:13
  28.9 0.0 all-gather.7.cloned.1.call-update
  28.9 25.8 %all-gather.5.cloned.1.call-done = bf16[1024,1024]{0,1:T(8,128)(2,1)} async-done(((bf16[1024,64]{0,1:T(8,128)(2,1)}), bf16[1024,1024]{0,1:T(8,128)(2,1)}) %all-gather.5.cloned.1.call-update) | async-done | bytes 2097168 | tf_op jit(solution)/shard_map/all_gather | solution.py:11
  54.7 58.3 %all-gather.7.cloned.1.call-done = bf16[32,32,2048]{2,1,0:T(8,128)(2,1)} async-done(((bf16[4,32,2048]{2,1,0:T(8,128)(2,1)}), bf16[32,32,2048]{2,1,0:T(8,128)(2,1)}) %all-gather.7.cloned.1.call-update) | async-done | bytes 4194320 | tf_op jit(solution)/shard_map/all_gather | solution.py:14
  113.0 9.4 %bitcast_convert_fusion = bf16[1024,2048]{1,0:T(8,128)(2,1)} fusion(bf16[8,4,32,2048]{3,2,1,0:T(8,128)(2,1)} %bitcast.9, bf16[1024,4,8,32]{0,3,2,1:T(8,128)(2,1)} %bitcast.10), kind=kOutput, calls=%fused_computation | convolution fusion | flops 4297064448 | bytes 10485760 | tf_op jit(solution)/shard_map/rzyk,yzkc->rc/dot_general | solution.py:16
Async XLA Ops:
  6.5 48.2 %all-gather.5.cloned.1.call-start = ((), (), s32[]{:S(2)}) async-start(), calls=%async_computation | async-start | bytes 2228224 | tf_op jit(solution)/shard_map/all_gather | solution.py:11
  7.3 105.7 %all-gather.7.cloned.1.call-start = ((), (), s32[]{:S(2)}) async-start(), calls=%async_computation.1 | async-start | bytes 4718592 | tf_op jit(solution)/shard_map/all_gather | solution.py:14
Sparse Core Ops, SparseCore 0:
  9.5 45.1 all-gather.4
  56.8 56.1 all-gather.6

commit v2 on v1

v2 whole, which is shorter than its diff:
```python
import jax
import jax.numpy as jnp
from jax import lax
from jax.sharding import Mesh, PartitionSpec as P

ROW = ("z_hi", "y")
COL = ("x", "z_lo", "core")


def swap(a, axis, cat):
    o = lax.ppermute(a, axis, [(0, 1), (1, 0)])
    first = lax.axis_index(axis) == 0
    return jnp.where(first, jnp.concatenate([a, o], cat), jnp.concatenate([o, a], cat))


def ring(a, axis, n):
    parts = [a] + [lax.ppermute(a, axis, [(i, (i - d) % n) for i in range(n)]) for d in range(1, n)]
    return jnp.roll(jnp.stack(parts), lax.axis_index(axis), axis=0)


def GZ(a):
    return lax.all_gather(a, "z_hi", axis=0, tiled=False)


def shards(s_rows, iterate):
    nx, nz, ny = lax.axis_size("x"), lax.axis_size("z_hi"), lax.axis_size("y")
    s = swap(s_rows, "core", 1)
    s = swap(s, "z_lo", 1)
    s = ring(s, "x", nx)
    w = GZ(iterate)
    w = lax.all_gather(w, "y", axis=0, tiled=False)
    s4 = s.reshape(nx, s.shape[1], ny, -1)
    product = jnp.einsum("zryk,yzkc->rc", s4, w, preferred_element_type=jnp.float32)
    return product.astype(jnp.bfloat16)


def solution(mesh):
    nr, nc = mesh.devices.shape
    devs = mesh.devices.reshape(4, nr // 4, nc // 4, 2, 2)
    m = Mesh(devs, ROW + COL)
    return jax.shard_map(shards, mesh=m, in_specs=(P(ROW, COL), P(ROW, COL)), out_specs=P(ROW, COL), check_vma=False)
```

time: 129 us -> 103 us (0.80)
  waiting for transfers between devices: 84.8 us -> 38.7 us
  starting transfers between devices: 0.04 us -> 18.4 us
  other arithmetic: 0 us -> 1.44 us
    all_gather x1, waiting for transfers between devices: 58.3 us -> 7.79 us  [shards(): w = lax.all_gather(w, 'y', axis=0, tiled=False)]
    ppermute x0 -> x5, waiting for transfers between devices: none -> 30.9 us  [the longest x3 23.4 us: ring(): lax.ppermute(a, axis, [(i, (i - d) % n) for i in range(n)])]
    all_gather x1 -> x0, waiting for transfers between devices: 25.8 us -> none  [shards(): panel = lax.all_gather(s_rows, COL, axis=1, tiled=True)]
    ppermute x0 -> x5, starting transfers between devices: none -> 18.4 us  [the longest x3 9.33 us: ring(): lax.ppermute(a, axis, [(i, (i - d) % n) for i in range(n)])]
  transfers between devices with their start and end apart: 2 -> 6, of which waited for: 2 -> 6; matrix products, arithmetic and copies ran while one was open for 0% -> 2% of each run, Pallas kernels for 0% -> 0%
where the time goes in v2:
time: 103 us; the launch traced here: 102 us
  waiting for transfers between devices  38.7 us (38%)
  blocking collectives  21.6 us (21%)
  starting transfers between devices  18.4 us (18%)
  between operations  13.5 us (13%)
  matrix products  8.31 us (8%)
  other arithmetic  1.44 us (1%)
    ppermute x3, waiting for transfers between devices, ring(): lax.ppermute(a, axis, [(i, (i - d) % n) for i in range(n)])  23.4 us
    all_gather x1, blocking collectives, GZ(): return lax.all_gather(a, 'z_hi', axis=0, tiled=False)  21.6 us
    ppermute x3, starting transfers between devices, ring(): lax.ppermute(a, axis, [(i, (i - d) % n) for i in range(n)])  9.33 us
    ppermute x2, starting transfers between devices, swap(): o = lax.ppermute(a, axis, [(0, 1), (1, 0)])  9.06 us
    dot_general x1, matrix products, shards(): jnp.einsum('zryk,yzkc->rc', s4, w, preferred_element_type=jnp.float32)  8.31 us
    all_gather x1, waiting for transfers between devices, shards(): w = lax.all_gather(w, 'y', axis=0, tiled=False)  7.79 us
    ppermute x2, waiting for transfers between devices, swap(): o = lax.ppermute(a, axis, [(0, 1), (1, 0)])  7.47 us
  transfers between devices with their start and end apart: 6, of which 6 were waited for; matrix products, arithmetic and copies ran while one was open for 2% of the time, Pallas kernels for 0%

profile of v2, /device:TPU:1, one launch (start us, length us, event | category | flops | bytes accessed | tf_op | source)
XLA Modules:
  0.0 102.3 jit_solution(8441944224514525163)
XLA Ops:
  6.5 0.0 all-gather.4.cloned.1.call-start
  6.5 21.6 %all-gather = bf16[128,2048]{1,0:T(8,128)(2,1)} all-gather(bf16[32,2048]{1,0:T(8,128)(2,1)} %param.3), channel_id=2, replica_groups=mesh['z_hi'=4,'y'=8,'x'=4,'z_lo'=2,'core'=2] {'z_hi'}, dimensions={0}, use_global_device_ids=true | all-gather | bytes 655360 | tf_op jit(solution)/shard_map/all_gather | solution.py:22
  28.1 0.0 all-gather.4.cloned.1.call-update
  28.1 4.3 %collective-permute-start = (bf16[1024,64]{0,1:T(8,128)(2,1)}, bf16[1024,64]{0,1:T(8,128)(2,1)S(1)}, u32[]{:S(2)}, u32[]{:S(2)}) collective-permute-start(bf16[1024,64]{0,1:T(8,128)(2,1)} %param.2), channel_id=1, source_target_pairs={{0,1},{1,0},{2,3},{3,2},{4,5},{5,4},{6,7},{7,6},{8,9},{9,8},{10,11... | collective-permute-start | bytes 393224 | tf_op jit(solution)/shard_map/ppermute | solution.py:11
  32.4 1.2 %collective-permute-done = bf16[1024,64]{0,1:T(8,128)(2,1)S(1)} collective-permute-done((bf16[1024,64]{0,1:T(8,128)(2,1)}, bf16[1024,64]{0,1:T(8,128)(2,1)S(1)}, u32[]{:S(2)}, u32[]{:S(2)}) %collective-permute-start) | collective-permute-done | bytes 131104 | tf_op jit(solution)/shard_map/ppermute | solution.py:11
  33.6 1.0 %maximum_select_fusion.2 = bf16[1024,128]{0,1:T(8,128)(2,1)S(1)} fusion(bf16[1024,64]{0,1:T(8,128)(2,1)S(1)} %collective-permute-done, bf16[1024,64]{0,1:T(8,128)(2,1)} %param.2, pred[]{:T(512)S(6)} %eq.10), kind=kLoop, calls=%fused_computation.10 | loop fusion | flops 1179648 | bytes 524289 | tf_op jit(solution)/shard_map/jit(_where)/select_n | solution.py:13
  34.6 4.8 %collective-permute-start.1 = (bf16[1024,128]{0,1:T(8,128)(2,1)S(1)}, bf16[1024,128]{0,1:T(8,128)(2,1)S(1)}, u32[]{:S(2)}, u32[]{:S(2)}) collective-permute-start(bf16[1024,128]{0,1:T(8,128)(2,1)S(1)} %maximum_select_fusion.2), channel_id=1, source_target_pairs={{0,2},{2,0},{1,3},{3,1},{4,6},{6,4},{5,7},{7,5},{8,10},{10,8},{9,1... | collective-permute-start | bytes 786440 | tf_op jit(solution)/shard_map/ppermute | solution.py:11
  39.4 6.3 %collective-permute-done.1 = bf16[1024,128]{0,1:T(8,128)(2,1)S(1)} collective-permute-done((bf16[1024,128]{0,1:T(8,128)(2,1)S(1)}, bf16[1024,128]{0,1:T(8,128)(2,1)S(1)}, u32[]{:S(2)}, u32[]{:S(2)}) %collective-permute-start.1) | collective-permute-done | bytes 262176 | tf_op jit(solution)/shard_map/ppermute | solution.py:11
  45.7 0.1 maximum_select_fusion.1
  45.9 4.4 %collective-permute-start.2 = (bf16[1024,256]{0,1:T(8,128)(2,1)S(1)}, bf16[1024,256]{0,1:T(8,128)(2,1)S(1)}, u32[]{:S(2)}, u32[]{:S(2)}) collective-permute-start(bf16[1024,256]{0,1:T(8,128)(2,1)S(1)} %maximum_select_fusion.1), channel_id=1, source_target_pairs={{0,12},{4,0},{8,4},{12,8},{1,13},{5,1},{9,5},{13,9},{2,14},{6,2},{... | collective-permute-start | bytes 1572872 | tf_op jit(solution)/shard_map/ppermute | solution.py:17
  50.3 2.4 %collective-permute-start.3 = (bf16[1024,256]{0,1:T(8,128)(2,1)S(1)}, bf16[1024,256]{0,1:T(8,128)(2,1)S(1)}, u32[]{:S(2)}, u32[]{:S(2)}) collective-permute-start(bf16[1024,256]{0,1:T(8,128)(2,1)S(1)} %maximum_select_fusion.1), channel_id=1, source_target_pairs={{0,8},{4,12},{8,0},{12,4},{1,9},{5,13},{9,1},{13,5},{2,10},{6,14},... | collective-permute-start | bytes 1572872 | tf_op jit(solution)/shard_map/ppermute | solution.py:17
  52.7 2.5 %collective-permute-start.4 = (bf16[1024,256]{0,1:T(8,128)(2,1)S(1)}, bf16[1024,256]{0,1:T(8,128)(2,1)S(1)}, u32[]{:S(2)}, u32[]{:S(2)}) collective-permute-start(bf16[1024,256]{0,1:T(8,128)(2,1)S(1)} %maximum_select_fusion.1), channel_id=1, source_target_pairs={{0,4},{4,8},{8,12},{12,0},{1,5},{5,9},{9,13},{13,1},{2,6},{6,10},{... | collective-permute-start | bytes 1572872 | tf_op jit(solution)/shard_map/ppermute | solution.py:17
  55.2 0.1 fusion.1
  55.4 6.0 %collective-permute-done.2 = bf16[1024,256]{0,1:T(8,128)(2,1)S(1)} collective-permute-done((bf16[1024,256]{0,1:T(8,128)(2,1)S(1)}, bf16[1024,256]{0,1:T(8,128)(2,1)S(1)}, u32[]{:S(2)}, u32[]{:S(2)}) %collective-permute-start.2) | collective-permute-done | bytes 524320 | tf_op jit(solution)/shard_map/ppermute | solution.py:17
  61.4 4.5 %collective-permute-done.3 = bf16[1024,256]{0,1:T(8,128)(2,1)S(1)} collective-permute-done((bf16[1024,256]{0,1:T(8,128)(2,1)S(1)}, bf16[1024,256]{0,1:T(8,128)(2,1)S(1)}, u32[]{:S(2)}, u32[]{:S(2)}) %collective-permute-start.3) | collective-permute-done | bytes 524320 | tf_op jit(solution)/shard_map/ppermute | solution.py:17
  66.0 12.8 %collective-permute-done.4 = bf16[1024,256]{0,1:T(8,128)(2,1)S(1)} collective-permute-done((bf16[1024,256]{0,1:T(8,128)(2,1)S(1)}, bf16[1024,256]{0,1:T(8,128)(2,1)S(1)}, u32[]{:S(2)}, u32[]{:S(2)}) %collective-permute-start.4) | collective-permute-done | bytes 524320 | tf_op jit(solution)/shard_map/ppermute | solution.py:17
  78.9 0.1 fusion.2
  79.2 0.2 constant_dynamic-slice_fusion
  79.3 7.8 %all-gather.4.cloned.1.call-done = bf16[32,32,2048]{2,1,0:T(8,128)(2,1)} async-done(((bf16[4,32,2048]{2,1,0:T(8,128)(2,1)}), bf16[32,32,2048]{2,1,0:T(8,128)(2,1)}) %all-gather.4.cloned.1.call-update) | async-done | bytes 4194320 | tf_op jit(solution)/shard_map/all_gather | solution.py:31
  87.1 8.3 %bitcast_convert_fusion = bf16[1024,2048]{1,0:T(8,128)(2,1)} fusion(bf16[8,4,32,2048]{3,2,1,0:T(8,128)(2,1)} %bitcast.25, bf16[4,1024,8,32]{1,3,2,0:T(8,128)(2,1)S(1)} %bitcast.24), kind=kOutput, calls=%fused_computation | convolution fusion | flops 4297064448 | bytes 10485760 | tf_op jit(solution)/shard_map/zryk,yzkc->rc/dot_general | solution.py:33
  (6 shorter events, 0.2 us)
Async XLA Ops:
  6.5 80.6 %all-gather.4.cloned.1.call-start = ((), (), s32[]{:S(2)}) async-start(), calls=%async_computation | async-start | bytes 4718592 | tf_op jit(solution)/shard_map/all_gather | solution.py:31
  28.1 5.5 %collective-permute-start = (bf16[1024,64]{0,1:T(8,128)(2,1)}, bf16[1024,64]{0,1:T(8,128)(2,1)S(1)}, u32[]{:S(2)}, u32[]{:S(2)}) collective-permute-start(bf16[1024,64]{0,1:T(8,128)(2,1)} %param.2), channel_id=1, source_target_pairs={{0,1},{1,0},{2,3},{3,2},{4,5},{5,4},{6,7},{7,6},{8,9},{9,8},{10,11... | collective-permute-start | bytes 393224 | tf_op jit(solution)/shard_map/ppermute | solution.py:11
  34.6 11.1 %collective-permute-start.1 = (bf16[1024,128]{0,1:T(8,128)(2,1)S(1)}, bf16[1024,128]{0,1:T(8,128)(2,1)S(1)}, u32[]{:S(2)}, u32[]{:S(2)}) collective-permute-start(bf16[1024,128]{0,1:T(8,128)(2,1)S(1)} %maximum_select_fusion.2), channel_id=1, source_target_pairs={{0,2},{2,0},{1,3},{3,1},{4,6},{6,4},{5,7},{7,5},{8,10},{10,8},{9,1... | collective-permute-start | bytes 786440 | tf_op jit(solution)/shard_map/ppermute | solution.py:11
  45.9 15.5 %collective-permute-start.2 = (bf16[1024,256]{0,1:T(8,128)(2,1)S(1)}, bf16[1024,256]{0,1:T(8,128)(2,1)S(1)}, u32[]{:S(2)}, u32[]{:S(2)}) collective-permute-start(bf16[1024,256]{0,1:T(8,128)(2,1)S(1)} %maximum_select_fusion.1), channel_id=1, source_target_pairs={{0,12},{4,0},{8,4},{12,8},{1,13},{5,1},{9,5},{13,9},{2,14},{6,2},{... | collective-permute-start | bytes 1572872 | tf_op jit(solution)/shard_map/ppermute | solution.py:17
  50.3 15.7 %collective-permute-start.3 = (bf16[1024,256]{0,1:T(8,128)(2,1)S(1)}, bf16[1024,256]{0,1:T(8,128)(2,1)S(1)}, u32[]{:S(2)}, u32[]{:S(2)}) collective-permute-start(bf16[1024,256]{0,1:T(8,128)(2,1)S(1)} %maximum_select_fusion.1), channel_id=1, source_target_pairs={{0,8},{4,12},{8,0},{12,4},{1,9},{5,13},{9,1},{13,5},{2,10},{6,14},... | collective-permute-start | bytes 1572872 | tf_op jit(solution)/shard_map/ppermute | solution.py:17
  52.7 26.1 %collective-permute-start.4 = (bf16[1024,256]{0,1:T(8,128)(2,1)S(1)}, bf16[1024,256]{0,1:T(8,128)(2,1)S(1)}, u32[]{:S(2)}, u32[]{:S(2)}) collective-permute-start(bf16[1024,256]{0,1:T(8,128)(2,1)S(1)} %maximum_select_fusion.1), channel_id=1, source_target_pairs={{0,4},{4,8},{8,12},{12,0},{1,5},{5,9},{9,13},{13,1},{2,6},{6,10},{... | collective-permute-start | bytes 1572872 | tf_op jit(solution)/shard_map/ppermute | solution.py:17
Sparse Core Ops, SparseCore 0:
  28.2 58.8 all-gather.3

commit v3 on v2

--- a/solution.py
+++ b/solution.py
@@ -1,6 +1,8 @@
 import jax
 import jax.numpy as jnp
 from jax import lax
+from jax.experimental import pallas as pl
+from jax.experimental.pallas import tpu as pltpu
 from jax.sharding import Mesh, PartitionSpec as P
 
 ROW = ("z_hi", "y")
@@ -22,6 +24,24 @@
     return lax.all_gather(a, "z_hi", axis=0, tiled=False)
 
 
+def mm_kernel(a_ref, b_ref, o_ref):
+    o_ref[...] = jnp.dot(a_ref[...], b_ref[...], preferred_element_type=jnp.float32).astype(o_ref.dtype)
+
+
+def matmul(a, b, tm=1024, tn=512):
+    m, k = a.shape
+    n = b.shape[1]
+    return pl.pallas_call(
+        mm_kernel,
+        out_shape=jax.ShapeDtypeStruct((m, n), jnp.bfloat16),
+        grid=(n // tn, m // tm),
+        in_specs=[pl.BlockSpec((tm, k), lambda j, i: (i, 0)), pl.BlockSpec((k, tn), lambda j, i: (0, j))],
+        out_specs=pl.BlockSpec((tm, tn), lambda j, i: (i, j)),
+        compiler_params=pltpu.CompilerParams(vmem_limit_bytes=48 * 1024 * 1024),
+        cost_estimate=pl.CostEstimate(flops=2 * m * n * k, bytes_accessed=2 * (m * k + k * n + m * n), transcendentals=0),
+    )(a, b)
+
+
 def shards(s_rows, iterate):
     nx, nz, ny = lax.axis_size("x"), lax.axis_size("z_hi"), lax.axis_size("y")
     s = swap(s_rows, "core", 1)
@@ -29,9 +49,9 @@
     s = ring(s, "x", nx)
     w = GZ(iterate)
     w = lax.all_gather(w, "y", axis=0, tiled=False)
-    s4 = s.reshape(nx, s.shape[1], ny, -1)
-    product = jnp.einsum("zryk,yzkc->rc", s4, w, preferred_element_type=jnp.float32)
-    return product.astype(jnp.bfloat16)
+    R = s.shape[1]
+    panel = jnp.transpose(s.reshape(nx, R, ny, -1), (1, 2, 0, 3)).reshape(R, -1)
+    return matmul(panel, w.reshape(-1, w.shape[-1]))
 
 
 def solution(mesh):

time: 103 us -> 102 us (level)
  matrix products: 8.31 us -> 0 us
  Pallas kernels: 0 us -> 7.64 us
  waiting for transfers between devices: 38.7 us -> 34.3 us
  local copies, waits for them, and re-layouts: 0.39 us -> 4.74 us
    dot_general x1 -> x0, matrix products: 8.31 us -> none  [shards(): jnp.einsum('zryk,yzkc->rc', s4, w, preferred_element_type=jnp.float32)]
    pallas_call x0 -> x1, Pallas kernels: none -> 7.64 us  [matmul(): pl.pallas_call(mm_kernel, out_shape=jax.ShapeDtypeStruct((m, n), jnp.bflo...]
    all_gather x1, waiting for transfers between devices: 7.79 us -> 3.44 us  [shards(): w = lax.all_gather(w, 'y', axis=0, tiled=False)]
    reshape x0 -> x1, local copies, waits for them, and re-layouts: none -> 2.85 us  [shards(): panel = jnp.transpose(s.reshape(nx, R, ny, -1), (1, 2, 0, 3)).reshape(R, -1)]
    transpose x0 -> x1, local copies, waits for them, and re-layouts: none -> 1.49 us  [shards(): panel = jnp.transpose(s.reshape(nx, R, ny, -1), (1, 2, 0, 3)).reshape(R, -1)]
  transfers between devices with their start and end apart: 6 -> 6, of which waited for: 6 -> 6; matrix products, arithmetic and copies ran while one was open for 2% -> 6% of each run, Pallas kernels for 0% -> 0%
where the time goes in v3:
time: 102 us
  waiting for transfers between devices  34.3 us (34%)
  blocking collectives  21.6 us (21%)
  starting transfers between devices  18.4 us (18%)
  between operations  13.5 us (13%)
  Pallas kernels  7.64 us (7%)
  local copies, waits for them, and re-layouts  4.74 us (5%)
  other arithmetic  1.44 us (1%)
    ppermute x3, waiting for transfers between devices, ring(): lax.ppermute(a, axis, [(i, (i - d) % n) for i in range(n)])  23.4 us
    all_gather x1, blocking collectives, GZ(): return lax.all_gather(a, 'z_hi', axis=0, tiled=False)  21.6 us
    ppermute x3, starting transfers between devices, ring(): lax.ppermute(a, axis, [(i, (i - d) % n) for i in range(n)])  9.33 us
    ppermute x2, starting transfers between devices, swap(): o = lax.ppermute(a, axis, [(0, 1), (1, 0)])  9.06 us
    pallas_call x1, Pallas kernels, matmul(): pl.pallas_call(mm_kernel, out_shape=jax.ShapeDtypeStruct((m, n), jnp.bflo...  7.64 us
    ppermute x2, waiting for transfers between devices, swap(): o = lax.ppermute(a, axis, [(0, 1), (1, 0)])  7.47 us
    all_gather x1, waiting for transfers between devices, shards(): w = lax.all_gather(w, 'y', axis=0, tiled=False)  3.44 us
    reshape x1, local copies, waits for them, and re-layouts, shards(): panel = jnp.transpose(s.reshape(nx, R, ny, -1), (1, 2, 0, 3)).reshape(R, -1)  2.85 us
  transfers between devices with their start and end apart: 6, of which 6 were waited for; matrix products, arithmetic and copies ran while one was open for 6% of the time, Pallas kernels for 0%

profile of v3, /device:TPU:1, one launch (start us, length us, event | category | flops | bytes accessed | tf_op | source)
XLA Modules:
  0.0 101.6 jit_solution(15397553104562393435)
XLA Ops:
  6.5 0.0 all-gather.4.cloned.1.call-start
  6.5 21.6 %all-gather = bf16[128,2048]{1,0:T(8,128)(2,1)} all-gather(bf16[32,2048]{1,0:T(8,128)(2,1)} %param.3), channel_id=2, replica_groups=mesh['z_hi'=4,'y'=8,'x'=4,'z_lo'=2,'core'=2] {'z_hi'}, dimensions={0}, use_global_device_ids=true | all-gather | bytes 655360 | tf_op jit(solution)/shard_map/all_gather | solution.py:24
  28.1 0.0 all-gather.4.cloned.1.call-update
  28.1 4.3 %collective-permute-start = (bf16[1024,64]{0,1:T(8,128)(2,1)}, bf16[1024,64]{0,1:T(8,128)(2,1)S(1)}, u32[]{:S(2)}, u32[]{:S(2)}) collective-permute-start(bf16[1024,64]{0,1:T(8,128)(2,1)} %param.2), channel_id=1, source_target_pairs={{0,1},{1,0},{2,3},{3,2},{4,5},{5,4},{6,7},{7,6},{8,9},{9,8},{10,11... | collective-permute-start | bytes 393224 | tf_op jit(solution)/shard_map/ppermute | solution.py:13
  32.4 1.2 %collective-permute-done = bf16[1024,64]{0,1:T(8,128)(2,1)S(1)} collective-permute-done((bf16[1024,64]{0,1:T(8,128)(2,1)}, bf16[1024,64]{0,1:T(8,128)(2,1)S(1)}, u32[]{:S(2)}, u32[]{:S(2)}) %collective-permute-start) | collective-permute-done | bytes 131104 | tf_op jit(solution)/shard_map/ppermute | solution.py:13
  33.6 1.0 %maximum_select_fusion.2 = bf16[1024,128]{0,1:T(8,128)(2,1)S(1)} fusion(bf16[1024,64]{0,1:T(8,128)(2,1)S(1)} %collective-permute-done, bf16[1024,64]{0,1:T(8,128)(2,1)} %param.2, pred[]{:T(512)S(6)} %eq.10), kind=kLoop, calls=%fused_computation.8 | loop fusion | flops 1179648 | bytes 524289 | tf_op jit(solution)/shard_map/jit(_where)/select_n | solution.py:15
  34.6 4.8 %collective-permute-start.1 = (bf16[1024,128]{0,1:T(8,128)(2,1)S(1)}, bf16[1024,128]{0,1:T(8,128)(2,1)S(1)}, u32[]{:S(2)}, u32[]{:S(2)}) collective-permute-start(bf16[1024,128]{0,1:T(8,128)(2,1)S(1)} %maximum_select_fusion.2), channel_id=1, source_target_pairs={{0,2},{2,0},{1,3},{3,1},{4,6},{6,4},{5,7},{7,5},{8,10},{10,8},{9,1... | collective-permute-start | bytes 786440 | tf_op jit(solution)/shard_map/ppermute | solution.py:13
  39.4 6.3 %collective-permute-done.1 = bf16[1024,128]{0,1:T(8,128)(2,1)S(1)} collective-permute-done((bf16[1024,128]{0,1:T(8,128)(2,1)S(1)}, bf16[1024,128]{0,1:T(8,128)(2,1)S(1)}, u32[]{:S(2)}, u32[]{:S(2)}) %collective-permute-start.1) | collective-permute-done | bytes 262176 | tf_op jit(solution)/shard_map/ppermute | solution.py:13
  45.7 0.1 maximum_select_fusion.1
  45.9 4.4 %collective-permute-start.2 = (bf16[1024,256]{0,1:T(8,128)(2,1)S(1)}, bf16[1024,256]{0,1:T(8,128)(2,1)S(1)}, u32[]{:S(2)}, u32[]{:S(2)}) collective-permute-start(bf16[1024,256]{0,1:T(8,128)(2,1)S(1)} %maximum_select_fusion.1), channel_id=1, source_target_pairs={{0,12},{4,0},{8,4},{12,8},{1,13},{5,1},{9,5},{13,9},{2,14},{6,2},{... | collective-permute-start | bytes 1572872 | tf_op jit(solution)/shard_map/ppermute | solution.py:19
  50.3 2.4 %collective-permute-start.3 = (bf16[1024,256]{0,1:T(8,128)(2,1)S(1)}, bf16[1024,256]{0,1:T(8,128)(2,1)S(1)}, u32[]{:S(2)}, u32[]{:S(2)}) collective-permute-start(bf16[1024,256]{0,1:T(8,128)(2,1)S(1)} %maximum_select_fusion.1), channel_id=1, source_target_pairs={{0,8},{4,12},{8,0},{12,4},{1,9},{5,13},{9,1},{13,5},{2,10},{6,14},... | collective-permute-start | bytes 1572872 | tf_op jit(solution)/shard_map/ppermute | solution.py:19
  52.7 2.5 %collective-permute-start.4 = (bf16[1024,256]{0,1:T(8,128)(2,1)S(1)}, bf16[1024,256]{0,1:T(8,128)(2,1)S(1)}, u32[]{:S(2)}, u32[]{:S(2)}) collective-permute-start(bf16[1024,256]{0,1:T(8,128)(2,1)S(1)} %maximum_select_fusion.1), channel_id=1, source_target_pairs={{0,4},{4,8},{8,12},{12,0},{1,5},{5,9},{9,13},{13,1},{2,6},{6,10},{... | collective-permute-start | bytes 1572872 | tf_op jit(solution)/shard_map/ppermute | solution.py:19
  55.2 0.1 fusion
  55.4 6.0 %collective-permute-done.2 = bf16[1024,256]{0,1:T(8,128)(2,1)S(1)} collective-permute-done((bf16[1024,256]{0,1:T(8,128)(2,1)S(1)}, bf16[1024,256]{0,1:T(8,128)(2,1)S(1)}, u32[]{:S(2)}, u32[]{:S(2)}) %collective-permute-start.2) | collective-permute-done | bytes 524320 | tf_op jit(solution)/shard_map/ppermute | solution.py:19
  61.4 4.5 %collective-permute-done.3 = bf16[1024,256]{0,1:T(8,128)(2,1)S(1)} collective-permute-done((bf16[1024,256]{0,1:T(8,128)(2,1)S(1)}, bf16[1024,256]{0,1:T(8,128)(2,1)S(1)}, u32[]{:S(2)}, u32[]{:S(2)}) %collective-permute-start.3) | collective-permute-done | bytes 524320 | tf_op jit(solution)/shard_map/ppermute | solution.py:19
  66.0 12.8 %collective-permute-done.4 = bf16[1024,256]{0,1:T(8,128)(2,1)S(1)} collective-permute-done((bf16[1024,256]{0,1:T(8,128)(2,1)S(1)}, bf16[1024,256]{0,1:T(8,128)(2,1)S(1)}, u32[]{:S(2)}, u32[]{:S(2)}) %collective-permute-start.4) | collective-permute-done | bytes 524320 | tf_op jit(solution)/shard_map/ppermute | solution.py:19
  78.9 0.1 fusion.1
  79.2 0.2 constant_dynamic-slice_fusion
  79.3 1.5 %copy.5 = bf16[1024,8,4,32]{0,3,2,1:T(8,128)(2,1)} copy(bf16[1024,8,4,32]{0,3,1,2:T(8,128)(2,1)S(1)} %bitcast.17) | data formatting | bytes 4194304 | tf_op jit(solution)/shard_map/transpose | solution.py:53
  80.8 2.9 %copy.6.a_ref = bf16[1024,1024]{1,0:T(8,128)(2,1)S(1)} copy(bf16[1024,1024]{0,1:T(8,128)(2,1)} %bitcast.18) | data formatting | bytes 4194304 | tf_op jit(solution)/shard_map/reshape | solution.py:53
  83.7 3.4 %all-gather.4.cloned.1.call-done = bf16[32,32,2048]{2,1,0:T(8,128)(2,1)} async-done(((bf16[4,32,2048]{2,1,0:T(8,128)(2,1)}), bf16[32,32,2048]{2,1,0:T(8,128)(2,1)}) %all-gather.4.cloned.1.call-update) | async-done | bytes 4194320 | tf_op jit(solution)/shard_map/all_gather | solution.py:51
  87.1 7.6 %shard_map.28 = bf16[1024,2048]{1,0:T(8,128)(2,1)} custom-call(bf16[1024,1024]{1,0:T(8,128)(2,1)S(1)} %copy.6.a_ref, bf16[1024,2048]{1,0:T(8,128)(2,1)} %bitcast.24), custom_call_target="tpu_custom_call" | custom-call | flops 4294967296 | bytes 10485760 | tf_op jit(solution)/shard_map/pallas_call | solution.py:34
  (6 shorter events, 0.2 us)
Async XLA Ops:
  6.5 80.6 %all-gather.4.cloned.1.call-start = ((), (), s32[]{:S(2)}) async-start(), calls=%async_computation | async-start | bytes 4718592 | tf_op jit(solution)/shard_map/all_gather | solution.py:51
  28.1 5.5 %collective-permute-start = (bf16[1024,64]{0,1:T(8,128)(2,1)}, bf16[1024,64]{0,1:T(8,128)(2,1)S(1)}, u32[]{:S(2)}, u32[]{:S(2)}) collective-permute-start(bf16[1024,64]{0,1:T(8,128)(2,1)} %param.2), channel_id=1, source_target_pairs={{0,1},{1,0},{2,3},{3,2},{4,5},{5,4},{6,7},{7,6},{8,9},{9,8},{10,11... | collective-permute-start | bytes 393224 | tf_op jit(solution)/shard_map/ppermute | solution.py:13
  34.6 11.1 %collective-permute-start.1 = (bf16[1024,128]{0,1:T(8,128)(2,1)S(1)}, bf16[1024,128]{0,1:T(8,128)(2,1)S(1)}, u32[]{:S(2)}, u32[]{:S(2)}) collective-permute-start(bf16[1024,128]{0,1:T(8,128)(2,1)S(1)} %maximum_select_fusion.2), channel_id=1, source_target_pairs={{0,2},{2,0},{1,3},{3,1},{4,6},{6,4},{5,7},{7,5},{8,10},{10,8},{9,1... | collective-permute-start | bytes 786440 | tf_op jit(solution)/shard_map/ppermute | solution.py:13
  45.9 15.5 %collective-permute-start.2 = (bf16[1024,256]{0,1:T(8,128)(2,1)S(1)}, bf16[1024,256]{0,1:T(8,128)(2,1)S(1)}, u32[]{:S(2)}, u32[]{:S(2)}) collective-permute-start(bf16[1024,256]{0,1:T(8,128)(2,1)S(1)} %maximum_select_fusion.1), channel_id=1, source_target_pairs={{0,12},{4,0},{8,4},{12,8},{1,13},{5,1},{9,5},{13,9},{2,14},{6,2},{... | collective-permute-start | bytes 1572872 | tf_op jit(solution)/shard_map/ppermute | solution.py:19
  50.3 15.7 %collective-permute-start.3 = (bf16[1024,256]{0,1:T(8,128)(2,1)S(1)}, bf16[1024,256]{0,1:T(8,128)(2,1)S(1)}, u32[]{:S(2)}, u32[]{:S(2)}) collective-permute-start(bf16[1024,256]{0,1:T(8,128)(2,1)S(1)} %maximum_select_fusion.1), channel_id=1, source_target_pairs={{0,8},{4,12},{8,0},{12,4},{1,9},{5,13},{9,1},{13,5},{2,10},{6,14},... | collective-permute-start | bytes 1572872 | tf_op jit(solution)/shard_map/ppermute | solution.py:19
  52.7 26.1 %collective-permute-start.4 = (bf16[1024,256]{0,1:T(8,128)(2,1)S(1)}, bf16[1024,256]{0,1:T(8,128)(2,1)S(1)}, u32[]{:S(2)}, u32[]{:S(2)}) collective-permute-start(bf16[1024,256]{0,1:T(8,128)(2,1)S(1)} %maximum_select_fusion.1), channel_id=1, source_target_pairs={{0,4},{4,8},{8,12},{12,0},{1,5},{5,9},{9,13},{13,1},{2,6},{6,10},{... | collective-permute-start | bytes 1572872 | tf_op jit(solution)/shard_map/ppermute | solution.py:19
Sparse Core Ops, SparseCore 0:
  28.2 58.8 all-gather.3

commit v4 on v3

--- a/solution.py
+++ b/solution.py
@@ -28,7 +28,7 @@
     o_ref[...] = jnp.dot(a_ref[...], b_ref[...], preferred_element_type=jnp.float32).astype(o_ref.dtype)
 
 
-def matmul(a, b, tm=1024, tn=512):
+def matmul(a, b, tm=1024, tn=256):
     m, k = a.shape
     n = b.shape[1]
     return pl.pallas_call(

time: 102 us -> 104 us (1.020)
  Pallas kernels: 7.64 us -> 9.25 us
    pallas_call x1, Pallas kernels: 7.64 us -> 9.25 us  [matmul(): pl.pallas_call(mm_kernel, out_shape=jax.ShapeDtypeStruct((m, n), jnp.bflo...]
where the time goes in v4:
time: 104 us; the launch traced here: 103 us
  waiting for transfers between devices  34.3 us (33%)
  blocking collectives  21.6 us (21%)
  starting transfers between devices  18.4 us (18%)
  between operations  13.5 us (13%)
  Pallas kernels  9.25 us (9%)
  local copies, waits for them, and re-layouts  4.74 us (5%)
  other arithmetic  1.44 us (1%)
    ppermute x3, waiting for transfers between devices, ring(): lax.ppermute(a, axis, [(i, (i - d) % n) for i in range(n)])  23.4 us
    all_gather x1, blocking collectives, GZ(): return lax.all_gather(a, 'z_hi', axis=0, tiled=False)  21.6 us
    ppermute x3, starting transfers between devices, ring(): lax.ppermute(a, axis, [(i, (i - d) % n) for i in range(n)])  9.33 us
    pallas_call x1, Pallas kernels, matmul(): pl.pallas_call(mm_kernel, out_shape=jax.ShapeDtypeStruct((m, n), jnp.bflo...  9.25 us
    ppermute x2, starting transfers between devices, swap(): o = lax.ppermute(a, axis, [(0, 1), (1, 0)])  9.06 us
    ppermute x2, waiting for transfers between devices, swap(): o = lax.ppermute(a, axis, [(0, 1), (1, 0)])  7.47 us
    all_gather x1, waiting for transfers between devices, shards(): w = lax.all_gather(w, 'y', axis=0, tiled=False)  3.44 us
    reshape x1, local copies, waits for them, and re-layouts, shards(): panel = jnp.transpose(s.reshape(nx, R, ny, -1), (1, 2, 0, 3)).reshape(R, -1)  2.85 us
  transfers between devices with their start and end apart: 6, of which 6 were waited for; matrix products, arithmetic and copies ran while one was open for 6% of the time, Pallas kernels for 0%

profile of v4, /device:TPU:1, one launch (start us, length us, event | category | flops | bytes accessed | tf_op | source)
XLA Modules:
  0.0 103.2 jit_solution(8041889781949017129)
XLA Ops:
  6.5 0.0 all-gather.4.cloned.1.call-start
  6.5 21.6 %all-gather = bf16[128,2048]{1,0:T(8,128)(2,1)} all-gather(bf16[32,2048]{1,0:T(8,128)(2,1)} %param.3), channel_id=2, replica_groups=mesh['z_hi'=4,'y'=8,'x'=4,'z_lo'=2,'core'=2] {'z_hi'}, dimensions={0}, use_global_device_ids=true | all-gather | bytes 655360 | tf_op jit(solution)/shard_map/all_gather | solution.py:24
  28.1 0.0 all-gather.4.cloned.1.call-update
  28.1 4.3 %collective-permute-start = (bf16[1024,64]{0,1:T(8,128)(2,1)}, bf16[1024,64]{0,1:T(8,128)(2,1)S(1)}, u32[]{:S(2)}, u32[]{:S(2)}) collective-permute-start(bf16[1024,64]{0,1:T(8,128)(2,1)} %param.2), channel_id=1, source_target_pairs={{0,1},{1,0},{2,3},{3,2},{4,5},{5,4},{6,7},{7,6},{8,9},{9,8},{10,11... | collective-permute-start | bytes 393224 | tf_op jit(solution)/shard_map/ppermute | solution.py:13
  32.4 1.2 %collective-permute-done = bf16[1024,64]{0,1:T(8,128)(2,1)S(1)} collective-permute-done((bf16[1024,64]{0,1:T(8,128)(2,1)}, bf16[1024,64]{0,1:T(8,128)(2,1)S(1)}, u32[]{:S(2)}, u32[]{:S(2)}) %collective-permute-start) | collective-permute-done | bytes 131104 | tf_op jit(solution)/shard_map/ppermute | solution.py:13
  33.6 1.0 %maximum_select_fusion.2 = bf16[1024,128]{0,1:T(8,128)(2,1)S(1)} fusion(bf16[1024,64]{0,1:T(8,128)(2,1)S(1)} %collective-permute-done, bf16[1024,64]{0,1:T(8,128)(2,1)} %param.2, pred[]{:T(512)S(6)} %eq.10), kind=kLoop, calls=%fused_computation.8 | loop fusion | flops 1179648 | bytes 524289 | tf_op jit(solution)/shard_map/jit(_where)/select_n | solution.py:15
  34.6 4.8 %collective-permute-start.1 = (bf16[1024,128]{0,1:T(8,128)(2,1)S(1)}, bf16[1024,128]{0,1:T(8,128)(2,1)S(1)}, u32[]{:S(2)}, u32[]{:S(2)}) collective-permute-start(bf16[1024,128]{0,1:T(8,128)(2,1)S(1)} %maximum_select_fusion.2), channel_id=1, source_target_pairs={{0,2},{2,0},{1,3},{3,1},{4,6},{6,4},{5,7},{7,5},{8,10},{10,8},{9,1... | collective-permute-start | bytes 786440 | tf_op jit(solution)/shard_map/ppermute | solution.py:13
  39.4 6.3 %collective-permute-done.1 = bf16[1024,128]{0,1:T(8,128)(2,1)S(1)} collective-permute-done((bf16[1024,128]{0,1:T(8,128)(2,1)S(1)}, bf16[1024,128]{0,1:T(8,128)(2,1)S(1)}, u32[]{:S(2)}, u32[]{:S(2)}) %collective-permute-start.1) | collective-permute-done | bytes 262176 | tf_op jit(solution)/shard_map/ppermute | solution.py:13
  45.7 0.1 maximum_select_fusion.1
  45.9 4.4 %collective-permute-start.2 = (bf16[1024,256]{0,1:T(8,128)(2,1)S(1)}, bf16[1024,256]{0,1:T(8,128)(2,1)S(1)}, u32[]{:S(2)}, u32[]{:S(2)}) collective-permute-start(bf16[1024,256]{0,1:T(8,128)(2,1)S(1)} %maximum_select_fusion.1), channel_id=1, source_target_pairs={{0,12},{4,0},{8,4},{12,8},{1,13},{5,1},{9,5},{13,9},{2,14},{6,2},{... | collective-permute-start | bytes 1572872 | tf_op jit(solution)/shard_map/ppermute | solution.py:19
  50.3 2.4 %collective-permute-start.3 = (bf16[1024,256]{0,1:T(8,128)(2,1)S(1)}, bf16[1024,256]{0,1:T(8,128)(2,1)S(1)}, u32[]{:S(2)}, u32[]{:S(2)}) collective-permute-start(bf16[1024,256]{0,1:T(8,128)(2,1)S(1)} %maximum_select_fusion.1), channel_id=1, source_target_pairs={{0,8},{4,12},{8,0},{12,4},{1,9},{5,13},{9,1},{13,5},{2,10},{6,14},... | collective-permute-start | bytes 1572872 | tf_op jit(solution)/shard_map/ppermute | solution.py:19
  52.7 2.5 %collective-permute-start.4 = (bf16[1024,256]{0,1:T(8,128)(2,1)S(1)}, bf16[1024,256]{0,1:T(8,128)(2,1)S(1)}, u32[]{:S(2)}, u32[]{:S(2)}) collective-permute-start(bf16[1024,256]{0,1:T(8,128)(2,1)S(1)} %maximum_select_fusion.1), channel_id=1, source_target_pairs={{0,4},{4,8},{8,12},{12,0},{1,5},{5,9},{9,13},{13,1},{2,6},{6,10},{... | collective-permute-start | bytes 1572872 | tf_op jit(solution)/shard_map/ppermute | solution.py:19
  55.2 0.1 fusion
  55.4 6.0 %collective-permute-done.2 = bf16[1024,256]{0,1:T(8,128)(2,1)S(1)} collective-permute-done((bf16[1024,256]{0,1:T(8,128)(2,1)S(1)}, bf16[1024,256]{0,1:T(8,128)(2,1)S(1)}, u32[]{:S(2)}, u32[]{:S(2)}) %collective-permute-start.2) | collective-permute-done | bytes 524320 | tf_op jit(solution)/shard_map/ppermute | solution.py:19
  61.4 4.5 %collective-permute-done.3 = bf16[1024,256]{0,1:T(8,128)(2,1)S(1)} collective-permute-done((bf16[1024,256]{0,1:T(8,128)(2,1)S(1)}, bf16[1024,256]{0,1:T(8,128)(2,1)S(1)}, u32[]{:S(2)}, u32[]{:S(2)}) %collective-permute-start.3) | collective-permute-done | bytes 524320 | tf_op jit(solution)/shard_map/ppermute | solution.py:19
  66.0 12.8 %collective-permute-done.4 = bf16[1024,256]{0,1:T(8,128)(2,1)S(1)} collective-permute-done((bf16[1024,256]{0,1:T(8,128)(2,1)S(1)}, bf16[1024,256]{0,1:T(8,128)(2,1)S(1)}, u32[]{:S(2)}, u32[]{:S(2)}) %collective-permute-start.4) | collective-permute-done | bytes 524320 | tf_op jit(solution)/shard_map/ppermute | solution.py:19
  78.9 0.1 fusion.1
  79.2 0.2 constant_dynamic-slice_fusion
  79.3 1.5 %copy.5 = bf16[1024,8,4,32]{0,3,2,1:T(8,128)(2,1)} copy(bf16[1024,8,4,32]{0,3,1,2:T(8,128)(2,1)S(1)} %bitcast.17) | data formatting | bytes 4194304 | tf_op jit(solution)/shard_map/transpose | solution.py:53
  80.8 2.9 %copy.6.a_ref = bf16[1024,1024]{1,0:T(8,128)(2,1)S(1)} copy(bf16[1024,1024]{0,1:T(8,128)(2,1)} %bitcast.18) | data formatting | bytes 4194304 | tf_op jit(solution)/shard_map/reshape | solution.py:53
  83.7 3.4 %all-gather.4.cloned.1.call-done = bf16[32,32,2048]{2,1,0:T(8,128)(2,1)} async-done(((bf16[4,32,2048]{2,1,0:T(8,128)(2,1)}), bf16[32,32,2048]{2,1,0:T(8,128)(2,1)}) %all-gather.4.cloned.1.call-update) | async-done | bytes 4194320 | tf_op jit(solution)/shard_map/all_gather | solution.py:51
  87.1 9.2 %shard_map.28 = bf16[1024,2048]{1,0:T(8,128)(2,1)} custom-call(bf16[1024,1024]{1,0:T(8,128)(2,1)S(1)} %copy.6.a_ref, bf16[1024,2048]{1,0:T(8,128)(2,1)} %bitcast.24), custom_call_target="tpu_custom_call" | custom-call | flops 4294967296 | bytes 10485760 | tf_op jit(solution)/shard_map/pallas_call | solution.py:34
  (6 shorter events, 0.2 us)
Async XLA Ops:
  6.5 80.6 %all-gather.4.cloned.1.call-start = ((), (), s32[]{:S(2)}) async-start(), calls=%async_computation | async-start | bytes 4718592 | tf_op jit(solution)/shard_map/all_gather | solution.py:51
  28.1 5.5 %collective-permute-start = (bf16[1024,64]{0,1:T(8,128)(2,1)}, bf16[1024,64]{0,1:T(8,128)(2,1)S(1)}, u32[]{:S(2)}, u32[]{:S(2)}) collective-permute-start(bf16[1024,64]{0,1:T(8,128)(2,1)} %param.2), channel_id=1, source_target_pairs={{0,1},{1,0},{2,3},{3,2},{4,5},{5,4},{6,7},{7,6},{8,9},{9,8},{10,11... | collective-permute-start | bytes 393224 | tf_op jit(solution)/shard_map/ppermute | solution.py:13
  34.6 11.1 %collective-permute-start.1 = (bf16[1024,128]{0,1:T(8,128)(2,1)S(1)}, bf16[1024,128]{0,1:T(8,128)(2,1)S(1)}, u32[]{:S(2)}, u32[]{:S(2)}) collective-permute-start(bf16[1024,128]{0,1:T(8,128)(2,1)S(1)} %maximum_select_fusion.2), channel_id=1, source_target_pairs={{0,2},{2,0},{1,3},{3,1},{4,6},{6,4},{5,7},{7,5},{8,10},{10,8},{9,1... | collective-permute-start | bytes 786440 | tf_op jit(solution)/shard_map/ppermute | solution.py:13
  45.9 15.5 %collective-permute-start.2 = (bf16[1024,256]{0,1:T(8,128)(2,1)S(1)}, bf16[1024,256]{0,1:T(8,128)(2,1)S(1)}, u32[]{:S(2)}, u32[]{:S(2)}) collective-permute-start(bf16[1024,256]{0,1:T(8,128)(2,1)S(1)} %maximum_select_fusion.1), channel_id=1, source_target_pairs={{0,12},{4,0},{8,4},{12,8},{1,13},{5,1},{9,5},{13,9},{2,14},{6,2},{... | collective-permute-start | bytes 1572872 | tf_op jit(solution)/shard_map/ppermute | solution.py:19
  50.3 15.7 %collective-permute-start.3 = (bf16[1024,256]{0,1:T(8,128)(2,1)S(1)}, bf16[1024,256]{0,1:T(8,128)(2,1)S(1)}, u32[]{:S(2)}, u32[]{:S(2)}) collective-permute-start(bf16[1024,256]{0,1:T(8,128)(2,1)S(1)} %maximum_select_fusion.1), channel_id=1, source_target_pairs={{0,8},{4,12},{8,0},{12,4},{1,9},{5,13},{9,1},{13,5},{2,10},{6,14},... | collective-permute-start | bytes 1572872 | tf_op jit(solution)/shard_map/ppermute | solution.py:19
  52.7 26.1 %collective-permute-start.4 = (bf16[1024,256]{0,1:T(8,128)(2,1)S(1)}, bf16[1024,256]{0,1:T(8,128)(2,1)S(1)}, u32[]{:S(2)}, u32[]{:S(2)}) collective-permute-start(bf16[1024,256]{0,1:T(8,128)(2,1)S(1)} %maximum_select_fusion.1), channel_id=1, source_target_pairs={{0,4},{4,8},{8,12},{12,0},{1,5},{5,9},{9,13},{13,1},{2,6},{6,10},{... | collective-permute-start | bytes 1572872 | tf_op jit(solution)/shard_map/ppermute | solution.py:19
Sparse Core Ops, SparseCore 0:
  28.2 58.8 all-gather.3

commit v5 on v4

--- a/solution.py
+++ b/solution.py
@@ -28,7 +28,7 @@
     o_ref[...] = jnp.dot(a_ref[...], b_ref[...], preferred_element_type=jnp.float32).astype(o_ref.dtype)
 
 
-def matmul(a, b, tm=1024, tn=256):
+def matmul(a, b, tm=1024, tn=1024):
     m, k = a.shape
     n = b.shape[1]
     return pl.pallas_call(

time: 104 us -> 102 us (0.981)
  Pallas kernels: 9.25 us -> 7.58 us
    pallas_call x1, Pallas kernels: 9.25 us -> 7.58 us  [matmul(): pl.pallas_call(mm_kernel, out_shape=jax.ShapeDtypeStruct((m, n), jnp.bflo...]
where the time goes in v5:
time: 102 us
  waiting for transfers between devices  34.3 us (34%)
  blocking collectives  21.6 us (21%)
  starting transfers between devices  18.4 us (18%)
  between operations  13.5 us (13%)
  Pallas kernels  7.58 us (7%)
  local copies, waits for them, and re-layouts  4.74 us (5%)
  other arithmetic  1.44 us (1%)
    ppermute x3, waiting for transfers between devices, ring(): lax.ppermute(a, axis, [(i, (i - d) % n) for i in range(n)])  23.4 us
    all_gather x1, blocking collectives, GZ(): return lax.all_gather(a, 'z_hi', axis=0, tiled=False)  21.6 us
    ppermute x3, starting transfers between devices, ring(): lax.ppermute(a, axis, [(i, (i - d) % n) for i in range(n)])  9.33 us
    ppermute x2, starting transfers between devices, swap(): o = lax.ppermute(a, axis, [(0, 1), (1, 0)])  9.06 us
    pallas_call x1, Pallas kernels, matmul(): pl.pallas_call(mm_kernel, out_shape=jax.ShapeDtypeStruct((m, n), jnp.bflo...  7.58 us
    ppermute x2, waiting for transfers between devices, swap(): o = lax.ppermute(a, axis, [(0, 1), (1, 0)])  7.47 us
    all_gather x1, waiting for transfers between devices, shards(): w = lax.all_gather(w, 'y', axis=0, tiled=False)  3.44 us
    reshape x1, local copies, waits for them, and re-layouts, shards(): panel = jnp.transpose(s.reshape(nx, R, ny, -1), (1, 2, 0, 3)).reshape(R, -1)  2.85 us
  transfers between devices with their start and end apart: 6, of which 6 were waited for; matrix products, arithmetic and copies ran while one was open for 6% of the time, Pallas kernels for 0%

profile of v5, /device:TPU:1, one launch (start us, length us, event | category | flops | bytes accessed | tf_op | source)
XLA Modules:
  0.0 101.6 jit_solution(17194161453153277237)
XLA Ops:
  6.5 0.0 all-gather.4.cloned.1.call-start
  6.5 21.6 %all-gather = bf16[128,2048]{1,0:T(8,128)(2,1)} all-gather(bf16[32,2048]{1,0:T(8,128)(2,1)} %param.3), channel_id=2, replica_groups=mesh['z_hi'=4,'y'=8,'x'=4,'z_lo'=2,'core'=2] {'z_hi'}, dimensions={0}, use_global_device_ids=true | all-gather | bytes 655360 | tf_op jit(solution)/shard_map/all_gather | solution.py:24
  28.1 0.0 all-gather.4.cloned.1.call-update
  28.1 4.3 %collective-permute-start = (bf16[1024,64]{0,1:T(8,128)(2,1)}, bf16[1024,64]{0,1:T(8,128)(2,1)S(1)}, u32[]{:S(2)}, u32[]{:S(2)}) collective-permute-start(bf16[1024,64]{0,1:T(8,128)(2,1)} %param.2), channel_id=1, source_target_pairs={{0,1},{1,0},{2,3},{3,2},{4,5},{5,4},{6,7},{7,6},{8,9},{9,8},{10,11... | collective-permute-start | bytes 393224 | tf_op jit(solution)/shard_map/ppermute | solution.py:13
  32.4 1.2 %collective-permute-done = bf16[1024,64]{0,1:T(8,128)(2,1)S(1)} collective-permute-done((bf16[1024,64]{0,1:T(8,128)(2,1)}, bf16[1024,64]{0,1:T(8,128)(2,1)S(1)}, u32[]{:S(2)}, u32[]{:S(2)}) %collective-permute-start) | collective-permute-done | bytes 131104 | tf_op jit(solution)/shard_map/ppermute | solution.py:13
  33.6 1.0 %maximum_select_fusion.2 = bf16[1024,128]{0,1:T(8,128)(2,1)S(1)} fusion(bf16[1024,64]{0,1:T(8,128)(2,1)S(1)} %collective-permute-done, bf16[1024,64]{0,1:T(8,128)(2,1)} %param.2, pred[]{:T(512)S(6)} %eq.10), kind=kLoop, calls=%fused_computation.8 | loop fusion | flops 1179648 | bytes 524289 | tf_op jit(solution)/shard_map/jit(_where)/select_n | solution.py:15
  34.6 4.8 %collective-permute-start.1 = (bf16[1024,128]{0,1:T(8,128)(2,1)S(1)}, bf16[1024,128]{0,1:T(8,128)(2,1)S(1)}, u32[]{:S(2)}, u32[]{:S(2)}) collective-permute-start(bf16[1024,128]{0,1:T(8,128)(2,1)S(1)} %maximum_select_fusion.2), channel_id=1, source_target_pairs={{0,2},{2,0},{1,3},{3,1},{4,6},{6,4},{5,7},{7,5},{8,10},{10,8},{9,1... | collective-permute-start | bytes 786440 | tf_op jit(solution)/shard_map/ppermute | solution.py:13
  39.4 6.3 %collective-permute-done.1 = bf16[1024,128]{0,1:T(8,128)(2,1)S(1)} collective-permute-done((bf16[1024,128]{0,1:T(8,128)(2,1)S(1)}, bf16[1024,128]{0,1:T(8,128)(2,1)S(1)}, u32[]{:S(2)}, u32[]{:S(2)}) %collective-permute-start.1) | collective-permute-done | bytes 262176 | tf_op jit(solution)/shard_map/ppermute | solution.py:13
  45.7 0.1 maximum_select_fusion.1
  45.9 4.4 %collective-permute-start.2 = (bf16[1024,256]{0,1:T(8,128)(2,1)S(1)}, bf16[1024,256]{0,1:T(8,128)(2,1)S(1)}, u32[]{:S(2)}, u32[]{:S(2)}) collective-permute-start(bf16[1024,256]{0,1:T(8,128)(2,1)S(1)} %maximum_select_fusion.1), channel_id=1, source_target_pairs={{0,12},{4,0},{8,4},{12,8},{1,13},{5,1},{9,5},{13,9},{2,14},{6,2},{... | collective-permute-start | bytes 1572872 | tf_op jit(solution)/shard_map/ppermute | solution.py:19
  50.3 2.4 %collective-permute-start.3 = (bf16[1024,256]{0,1:T(8,128)(2,1)S(1)}, bf16[1024,256]{0,1:T(8,128)(2,1)S(1)}, u32[]{:S(2)}, u32[]{:S(2)}) collective-permute-start(bf16[1024,256]{0,1:T(8,128)(2,1)S(1)} %maximum_select_fusion.1), channel_id=1, source_target_pairs={{0,8},{4,12},{8,0},{12,4},{1,9},{5,13},{9,1},{13,5},{2,10},{6,14},... | collective-permute-start | bytes 1572872 | tf_op jit(solution)/shard_map/ppermute | solution.py:19
  52.7 2.5 %collective-permute-start.4 = (bf16[1024,256]{0,1:T(8,128)(2,1)S(1)}, bf16[1024,256]{0,1:T(8,128)(2,1)S(1)}, u32[]{:S(2)}, u32[]{:S(2)}) collective-permute-start(bf16[1024,256]{0,1:T(8,128)(2,1)S(1)} %maximum_select_fusion.1), channel_id=1, source_target_pairs={{0,4},{4,8},{8,12},{12,0},{1,5},{5,9},{9,13},{13,1},{2,6},{6,10},{... | collective-permute-start | bytes 1572872 | tf_op jit(solution)/shard_map/ppermute | solution.py:19
  55.2 0.1 fusion
  55.4 6.0 %collective-permute-done.2 = bf16[1024,256]{0,1:T(8,128)(2,1)S(1)} collective-permute-done((bf16[1024,256]{0,1:T(8,128)(2,1)S(1)}, bf16[1024,256]{0,1:T(8,128)(2,1)S(1)}, u32[]{:S(2)}, u32[]{:S(2)}) %collective-permute-start.2) | collective-permute-done | bytes 524320 | tf_op jit(solution)/shard_map/ppermute | solution.py:19
  61.4 4.5 %collective-permute-done.3 = bf16[1024,256]{0,1:T(8,128)(2,1)S(1)} collective-permute-done((bf16[1024,256]{0,1:T(8,128)(2,1)S(1)}, bf16[1024,256]{0,1:T(8,128)(2,1)S(1)}, u32[]{:S(2)}, u32[]{:S(2)}) %collective-permute-start.3) | collective-permute-done | bytes 524320 | tf_op jit(solution)/shard_map/ppermute | solution.py:19
  66.0 12.8 %collective-permute-done.4 = bf16[1024,256]{0,1:T(8,128)(2,1)S(1)} collective-permute-done((bf16[1024,256]{0,1:T(8,128)(2,1)S(1)}, bf16[1024,256]{0,1:T(8,128)(2,1)S(1)}, u32[]{:S(2)}, u32[]{:S(2)}) %collective-permute-start.4) | collective-permute-done | bytes 524320 | tf_op jit(solution)/shard_map/ppermute | solution.py:19
  78.9 0.1 fusion.1
  79.2 0.2 constant_dynamic-slice_fusion
  79.3 1.5 %copy.5 = bf16[1024,8,4,32]{0,3,2,1:T(8,128)(2,1)} copy(bf16[1024,8,4,32]{0,3,1,2:T(8,128)(2,1)S(1)} %bitcast.17) | data formatting | bytes 4194304 | tf_op jit(solution)/shard_map/transpose | solution.py:53
  80.8 2.9 %copy.6.a_ref = bf16[1024,1024]{1,0:T(8,128)(2,1)S(1)} copy(bf16[1024,1024]{0,1:T(8,128)(2,1)} %bitcast.18) | data formatting | bytes 4194304 | tf_op jit(solution)/shard_map/reshape | solution.py:53
  83.7 3.4 %all-gather.4.cloned.1.call-done = bf16[32,32,2048]{2,1,0:T(8,128)(2,1)} async-done(((bf16[4,32,2048]{2,1,0:T(8,128)(2,1)}), bf16[32,32,2048]{2,1,0:T(8,128)(2,1)}) %all-gather.4.cloned.1.call-update) | async-done | bytes 4194320 | tf_op jit(solution)/shard_map/all_gather | solution.py:51
  87.1 7.6 %shard_map.28 = bf16[1024,2048]{1,0:T(8,128)(2,1)} custom-call(bf16[1024,1024]{1,0:T(8,128)(2,1)S(1)} %copy.6.a_ref, bf16[1024,2048]{1,0:T(8,128)(2,1)} %bitcast.24), custom_call_target="tpu_custom_call" | custom-call | flops 4294967296 | bytes 10485760 | tf_op jit(solution)/shard_map/pallas_call | solution.py:34
  (6 shorter events, 0.2 us)
Async XLA Ops:
  6.5 80.6 %all-gather.4.cloned.1.call-start = ((), (), s32[]{:S(2)}) async-start(), calls=%async_computation | async-start | bytes 4718592 | tf_op jit(solution)/shard_map/all_gather | solution.py:51
  28.1 5.5 %collective-permute-start = (bf16[1024,64]{0,1:T(8,128)(2,1)}, bf16[1024,64]{0,1:T(8,128)(2,1)S(1)}, u32[]{:S(2)}, u32[]{:S(2)}) collective-permute-start(bf16[1024,64]{0,1:T(8,128)(2,1)} %param.2), channel_id=1, source_target_pairs={{0,1},{1,0},{2,3},{3,2},{4,5},{5,4},{6,7},{7,6},{8,9},{9,8},{10,11... | collective-permute-start | bytes 393224 | tf_op jit(solution)/shard_map/ppermute | solution.py:13
  34.6 11.1 %collective-permute-start.1 = (bf16[1024,128]{0,1:T(8,128)(2,1)S(1)}, bf16[1024,128]{0,1:T(8,128)(2,1)S(1)}, u32[]{:S(2)}, u32[]{:S(2)}) collective-permute-start(bf16[1024,128]{0,1:T(8,128)(2,1)S(1)} %maximum_select_fusion.2), channel_id=1, source_target_pairs={{0,2},{2,0},{1,3},{3,1},{4,6},{6,4},{5,7},{7,5},{8,10},{10,8},{9,1... | collective-permute-start | bytes 786440 | tf_op jit(solution)/shard_map/ppermute | solution.py:13
  45.9 15.5 %collective-permute-start.2 = (bf16[1024,256]{0,1:T(8,128)(2,1)S(1)}, bf16[1024,256]{0,1:T(8,128)(2,1)S(1)}, u32[]{:S(2)}, u32[]{:S(2)}) collective-permute-start(bf16[1024,256]{0,1:T(8,128)(2,1)S(1)} %maximum_select_fusion.1), channel_id=1, source_target_pairs={{0,12},{4,0},{8,4},{12,8},{1,13},{5,1},{9,5},{13,9},{2,14},{6,2},{... | collective-permute-start | bytes 1572872 | tf_op jit(solution)/shard_map/ppermute | solution.py:19
  50.3 15.7 %collective-permute-start.3 = (bf16[1024,256]{0,1:T(8,128)(2,1)S(1)}, bf16[1024,256]{0,1:T(8,128)(2,1)S(1)}, u32[]{:S(2)}, u32[]{:S(2)}) collective-permute-start(bf16[1024,256]{0,1:T(8,128)(2,1)S(1)} %maximum_select_fusion.1), channel_id=1, source_target_pairs={{0,8},{4,12},{8,0},{12,4},{1,9},{5,13},{9,1},{13,5},{2,10},{6,14},... | collective-permute-start | bytes 1572872 | tf_op jit(solution)/shard_map/ppermute | solution.py:19
  52.7 26.1 %collective-permute-start.4 = (bf16[1024,256]{0,1:T(8,128)(2,1)S(1)}, bf16[1024,256]{0,1:T(8,128)(2,1)S(1)}, u32[]{:S(2)}, u32[]{:S(2)}) collective-permute-start(bf16[1024,256]{0,1:T(8,128)(2,1)S(1)} %maximum_select_fusion.1), channel_id=1, source_target_pairs={{0,4},{4,8},{8,12},{12,0},{1,5},{5,9},{9,13},{13,1},{2,6},{6,10},{... | collective-permute-start | bytes 1572872 | tf_op jit(solution)/shard_map/ppermute | solution.py:19
Sparse Core Ops, SparseCore 0:
  28.2 58.8 all-gather.3

commit v6 on v5

--- a/solution.py
+++ b/solution.py
@@ -28,7 +28,7 @@
     o_ref[...] = jnp.dot(a_ref[...], b_ref[...], preferred_element_type=jnp.float32).astype(o_ref.dtype)
 
 
-def matmul(a, b, tm=1024, tn=1024):
+def matmul(a, b, tm=512, tn=2048):
     m, k = a.shape
     n = b.shape[1]
     return pl.pallas_call(

time: 102 us -> 103 us (level)
  no operation moved by 1% of the time
where the time goes in v6:
time: 103 us; the launch traced here: 102 us
  waiting for transfers between devices  34.3 us (33%)
  blocking collectives  21.6 us (21%)
  starting transfers between devices  18.4 us (18%)
  between operations  13.5 us (13%)
  Pallas kernels  8.19 us (8%)
  local copies, waits for them, and re-layouts  4.74 us (5%)
  other arithmetic  1.44 us (1%)
    ppermute x3, waiting for transfers between devices, ring(): lax.ppermute(a, axis, [(i, (i - d) % n) for i in range(n)])  23.4 us
    all_gather x1, blocking collectives, GZ(): return lax.all_gather(a, 'z_hi', axis=0, tiled=False)  21.6 us
    ppermute x3, starting transfers between devices, ring(): lax.ppermute(a, axis, [(i, (i - d) % n) for i in range(n)])  9.33 us
    ppermute x2, starting transfers between devices, swap(): o = lax.ppermute(a, axis, [(0, 1), (1, 0)])  9.06 us
    pallas_call x1, Pallas kernels, matmul(): pl.pallas_call(mm_kernel, out_shape=jax.ShapeDtypeStruct((m, n), jnp.bflo...  8.19 us
    ppermute x2, waiting for transfers between devices, swap(): o = lax.ppermute(a, axis, [(0, 1), (1, 0)])  7.47 us
    all_gather x1, waiting for transfers between devices, shards(): w = lax.all_gather(w, 'y', axis=0, tiled=False)  3.44 us
    reshape x1, local copies, waits for them, and re-layouts, shards(): panel = jnp.transpose(s.reshape(nx, R, ny, -1), (1, 2, 0, 3)).reshape(R, -1)  2.85 us
  transfers between devices with their start and end apart: 6, of which 6 were waited for; matrix products, arithmetic and copies ran while one was open for 6% of the time, Pallas kernels for 0%

profile of v6, /device:TPU:1, one launch (start us, length us, event | category | flops | bytes accessed | tf_op | source)
XLA Modules:
  0.0 102.2 jit_solution(10513661434090818661)
XLA Ops:
  6.5 0.0 all-gather.4.cloned.1.call-start
  6.5 21.6 %all-gather = bf16[128,2048]{1,0:T(8,128)(2,1)} all-gather(bf16[32,2048]{1,0:T(8,128)(2,1)} %param.3), channel_id=2, replica_groups=mesh['z_hi'=4,'y'=8,'x'=4,'z_lo'=2,'core'=2] {'z_hi'}, dimensions={0}, use_global_device_ids=true | all-gather | bytes 655360 | tf_op jit(solution)/shard_map/all_gather | solution.py:24
  28.1 0.0 all-gather.4.cloned.1.call-update
  28.1 4.3 %collective-permute-start = (bf16[1024,64]{0,1:T(8,128)(2,1)}, bf16[1024,64]{0,1:T(8,128)(2,1)S(1)}, u32[]{:S(2)}, u32[]{:S(2)}) collective-permute-start(bf16[1024,64]{0,1:T(8,128)(2,1)} %param.2), channel_id=1, source_target_pairs={{0,1},{1,0},{2,3},{3,2},{4,5},{5,4},{6,7},{7,6},{8,9},{9,8},{10,11... | collective-permute-start | bytes 393224 | tf_op jit(solution)/shard_map/ppermute | solution.py:13
  32.4 1.2 %collective-permute-done = bf16[1024,64]{0,1:T(8,128)(2,1)S(1)} collective-permute-done((bf16[1024,64]{0,1:T(8,128)(2,1)}, bf16[1024,64]{0,1:T(8,128)(2,1)S(1)}, u32[]{:S(2)}, u32[]{:S(2)}) %collective-permute-start) | collective-permute-done | bytes 131104 | tf_op jit(solution)/shard_map/ppermute | solution.py:13
  33.6 1.0 %maximum_select_fusion.2 = bf16[1024,128]{0,1:T(8,128)(2,1)S(1)} fusion(bf16[1024,64]{0,1:T(8,128)(2,1)S(1)} %collective-permute-done, bf16[1024,64]{0,1:T(8,128)(2,1)} %param.2, pred[]{:T(512)S(6)} %eq.10), kind=kLoop, calls=%fused_computation.8 | loop fusion | flops 1179648 | bytes 524289 | tf_op jit(solution)/shard_map/jit(_where)/select_n | solution.py:15
  34.6 4.8 %collective-permute-start.1 = (bf16[1024,128]{0,1:T(8,128)(2,1)S(1)}, bf16[1024,128]{0,1:T(8,128)(2,1)S(1)}, u32[]{:S(2)}, u32[]{:S(2)}) collective-permute-start(bf16[1024,128]{0,1:T(8,128)(2,1)S(1)} %maximum_select_fusion.2), channel_id=1, source_target_pairs={{0,2},{2,0},{1,3},{3,1},{4,6},{6,4},{5,7},{7,5},{8,10},{10,8},{9,1... | collective-permute-start | bytes 786440 | tf_op jit(solution)/shard_map/ppermute | solution.py:13
  39.4 6.3 %collective-permute-done.1 = bf16[1024,128]{0,1:T(8,128)(2,1)S(1)} collective-permute-done((bf16[1024,128]{0,1:T(8,128)(2,1)S(1)}, bf16[1024,128]{0,1:T(8,128)(2,1)S(1)}, u32[]{:S(2)}, u32[]{:S(2)}) %collective-permute-start.1) | collective-permute-done | bytes 262176 | tf_op jit(solution)/shard_map/ppermute | solution.py:13
  45.7 0.1 maximum_select_fusion.1
  45.9 4.4 %collective-permute-start.2 = (bf16[1024,256]{0,1:T(8,128)(2,1)S(1)}, bf16[1024,256]{0,1:T(8,128)(2,1)S(1)}, u32[]{:S(2)}, u32[]{:S(2)}) collective-permute-start(bf16[1024,256]{0,1:T(8,128)(2,1)S(1)} %maximum_select_fusion.1), channel_id=1, source_target_pairs={{0,12},{4,0},{8,4},{12,8},{1,13},{5,1},{9,5},{13,9},{2,14},{6,2},{... | collective-permute-start | bytes 1572872 | tf_op jit(solution)/shard_map/ppermute | solution.py:19
  50.3 2.4 %collective-permute-start.3 = (bf16[1024,256]{0,1:T(8,128)(2,1)S(1)}, bf16[1024,256]{0,1:T(8,128)(2,1)S(1)}, u32[]{:S(2)}, u32[]{:S(2)}) collective-permute-start(bf16[1024,256]{0,1:T(8,128)(2,1)S(1)} %maximum_select_fusion.1), channel_id=1, source_target_pairs={{0,8},{4,12},{8,0},{12,4},{1,9},{5,13},{9,1},{13,5},{2,10},{6,14},... | collective-permute-start | bytes 1572872 | tf_op jit(solution)/shard_map/ppermute | solution.py:19
  52.7 2.5 %collective-permute-start.4 = (bf16[1024,256]{0,1:T(8,128)(2,1)S(1)}, bf16[1024,256]{0,1:T(8,128)(2,1)S(1)}, u32[]{:S(2)}, u32[]{:S(2)}) collective-permute-start(bf16[1024,256]{0,1:T(8,128)(2,1)S(1)} %maximum_select_fusion.1), channel_id=1, source_target_pairs={{0,4},{4,8},{8,12},{12,0},{1,5},{5,9},{9,13},{13,1},{2,6},{6,10},{... | collective-permute-start | bytes 1572872 | tf_op jit(solution)/shard_map/ppermute | solution.py:19
  55.2 0.1 fusion
  55.4 6.0 %collective-permute-done.2 = bf16[1024,256]{0,1:T(8,128)(2,1)S(1)} collective-permute-done((bf16[1024,256]{0,1:T(8,128)(2,1)S(1)}, bf16[1024,256]{0,1:T(8,128)(2,1)S(1)}, u32[]{:S(2)}, u32[]{:S(2)}) %collective-permute-start.2) | collective-permute-done | bytes 524320 | tf_op jit(solution)/shard_map/ppermute | solution.py:19
  61.4 4.5 %collective-permute-done.3 = bf16[1024,256]{0,1:T(8,128)(2,1)S(1)} collective-permute-done((bf16[1024,256]{0,1:T(8,128)(2,1)S(1)}, bf16[1024,256]{0,1:T(8,128)(2,1)S(1)}, u32[]{:S(2)}, u32[]{:S(2)}) %collective-permute-start.3) | collective-permute-done | bytes 524320 | tf_op jit(solution)/shard_map/ppermute | solution.py:19
  66.0 12.8 %collective-permute-done.4 = bf16[1024,256]{0,1:T(8,128)(2,1)S(1)} collective-permute-done((bf16[1024,256]{0,1:T(8,128)(2,1)S(1)}, bf16[1024,256]{0,1:T(8,128)(2,1)S(1)}, u32[]{:S(2)}, u32[]{:S(2)}) %collective-permute-start.4) | collective-permute-done | bytes 524320 | tf_op jit(solution)/shard_map/ppermute | solution.py:19
  78.9 0.1 fusion.1
  79.2 0.2 constant_dynamic-slice_fusion
  79.3 1.5 %copy.5 = bf16[1024,8,4,32]{0,3,2,1:T(8,128)(2,1)} copy(bf16[1024,8,4,32]{0,3,1,2:T(8,128)(2,1)S(1)} %bitcast.17) | data formatting | bytes 4194304 | tf_op jit(solution)/shard_map/transpose | solution.py:53
  80.8 2.9 %copy.6.a_ref = bf16[1024,1024]{1,0:T(8,128)(2,1)S(1)} copy(bf16[1024,1024]{0,1:T(8,128)(2,1)} %bitcast.18) | data formatting | bytes 4194304 | tf_op jit(solution)/shard_map/reshape | solution.py:53
  83.7 3.4 %all-gather.4.cloned.1.call-done = bf16[32,32,2048]{2,1,0:T(8,128)(2,1)} async-done(((bf16[4,32,2048]{2,1,0:T(8,128)(2,1)}), bf16[32,32,2048]{2,1,0:T(8,128)(2,1)}) %all-gather.4.cloned.1.call-update) | async-done | bytes 4194320 | tf_op jit(solution)/shard_map/all_gather | solution.py:51
  87.1 8.2 %shard_map.28 = bf16[1024,2048]{1,0:T(8,128)(2,1)} custom-call(bf16[1024,1024]{1,0:T(8,128)(2,1)S(1)} %copy.6.a_ref, bf16[1024,2048]{1,0:T(8,128)(2,1)} %bitcast.24), custom_call_target="tpu_custom_call" | custom-call | flops 4294967296 | bytes 10485760 | tf_op jit(solution)/shard_map/pallas_call | solution.py:34
  (6 shorter events, 0.2 us)
Async XLA Ops:
  6.5 80.6 %all-gather.4.cloned.1.call-start = ((), (), s32[]{:S(2)}) async-start(), calls=%async_computation | async-start | bytes 4718592 | tf_op jit(solution)/shard_map/all_gather | solution.py:51
  28.1 5.5 %collective-permute-start = (bf16[1024,64]{0,1:T(8,128)(2,1)}, bf16[1024,64]{0,1:T(8,128)(2,1)S(1)}, u32[]{:S(2)}, u32[]{:S(2)}) collective-permute-start(bf16[1024,64]{0,1:T(8,128)(2,1)} %param.2), channel_id=1, source_target_pairs={{0,1},{1,0},{2,3},{3,2},{4,5},{5,4},{6,7},{7,6},{8,9},{9,8},{10,11... | collective-permute-start | bytes 393224 | tf_op jit(solution)/shard_map/ppermute | solution.py:13
  34.6 11.1 %collective-permute-start.1 = (bf16[1024,128]{0,1:T(8,128)(2,1)S(1)}, bf16[1024,128]{0,1:T(8,128)(2,1)S(1)}, u32[]{:S(2)}, u32[]{:S(2)}) collective-permute-start(bf16[1024,128]{0,1:T(8,128)(2,1)S(1)} %maximum_select_fusion.2), channel_id=1, source_target_pairs={{0,2},{2,0},{1,3},{3,1},{4,6},{6,4},{5,7},{7,5},{8,10},{10,8},{9,1... | collective-permute-start | bytes 786440 | tf_op jit(solution)/shard_map/ppermute | solution.py:13
  45.9 15.5 %collective-permute-start.2 = (bf16[1024,256]{0,1:T(8,128)(2,1)S(1)}, bf16[1024,256]{0,1:T(8,128)(2,1)S(1)}, u32[]{:S(2)}, u32[]{:S(2)}) collective-permute-start(bf16[1024,256]{0,1:T(8,128)(2,1)S(1)} %maximum_select_fusion.1), channel_id=1, source_target_pairs={{0,12},{4,0},{8,4},{12,8},{1,13},{5,1},{9,5},{13,9},{2,14},{6,2},{... | collective-permute-start | bytes 1572872 | tf_op jit(solution)/shard_map/ppermute | solution.py:19
  50.3 15.7 %collective-permute-start.3 = (bf16[1024,256]{0,1:T(8,128)(2,1)S(1)}, bf16[1024,256]{0,1:T(8,128)(2,1)S(1)}, u32[]{:S(2)}, u32[]{:S(2)}) collective-permute-start(bf16[1024,256]{0,1:T(8,128)(2,1)S(1)} %maximum_select_fusion.1), channel_id=1, source_target_pairs={{0,8},{4,12},{8,0},{12,4},{1,9},{5,13},{9,1},{13,5},{2,10},{6,14},... | collective-permute-start | bytes 1572872 | tf_op jit(solution)/shard_map/ppermute | solution.py:19
  52.7 26.1 %collective-permute-start.4 = (bf16[1024,256]{0,1:T(8,128)(2,1)S(1)}, bf16[1024,256]{0,1:T(8,128)(2,1)S(1)}, u32[]{:S(2)}, u32[]{:S(2)}) collective-permute-start(bf16[1024,256]{0,1:T(8,128)(2,1)S(1)} %maximum_select_fusion.1), channel_id=1, source_target_pairs={{0,4},{4,8},{8,12},{12,0},{1,5},{5,9},{9,13},{13,1},{2,6},{6,10},{... | collective-permute-start | bytes 1572872 | tf_op jit(solution)/shard_map/ppermute | solution.py:19
Sparse Core Ops, SparseCore 0:
  28.2 58.8 all-gather.3
